TPU v7x, 32 devices: a whole 2x2x4 slice. The times are simulated.
32 devices in a mesh: parts: 2 (over y), tm: 4 (over x, core), cols: 4 (over z).
Axes of the slice: x: 2, y: 2, z: 4, core: 2. Of those that a mesh axis runs over, the one named last changes fastest.
Arguments:
- noise: float32 [16, 1024, 1024], P(('parts', 'tm'), None, 'cols'), parts along dimension 0, may hold values from -6 to 6
- inv_diag: float32 [16, 1024, 1024], P(('parts', 'tm'), None, 'cols'), parts along dimension 0, may hold values from -2 to 2, as said below
- coupling: float32 [16, 1024, 1024], P(('parts', 'tm'), None, 'cols'), parts along dimension 0, may hold values from -1 to 1, as said below
- order: int32 [1024], replicated, may hold values from 0 to 1023, each once
Outputs:
- sample: float32 [16, 1024, 1024], P(('parts', 'tm'), None, 'cols'), parts along dimension 0
There are 2 independent parts, one for each index of `parts`. A program takes and returns all parts, laid end to end along the dimension named above; an argument that names none is the same for every part. Nothing has to cross between parts.
Inputs may be any that keep to these rules, and one draw needn't show every extreme that they name: `order`: each of 0 to 1023 appears once. `inv_diag`: diagonal entries lie between 0.5 and 2, off-diagonal entries are small in magnitude. `coupling`: diagonal entries lie between 0.5 and 0.97, off-diagonal entries are small in magnitude.
All inputs are finite; a program needn't handle non-finite values.
Results may differ from a plain program's by a relative error of at most 0.00013.
Values sent between devices are 32-bit elements; how exact they have to be, the bound alone decides.
No kernel may reach another device: no remote copies, remote signals or barrier semaphores. Data moves between devices by JAX's collectives and lax.ppermute only.
A program may use at most 128 MiB of HBM per device.

v0:
```python
import jax
import jax.numpy as jnp
from jax import lax
from jax.sharding import PartitionSpec as P

low = jnp.bfloat16


def shifted(block, axis, distance):
    devices = range(lax.axis_size(axis))
    route = [(i - distance, i) for i in devices if i - distance in devices]
    return lax.ppermute(block, axis, route)


def split(value, count):
    parts = []
    rest = value
    for index in range(count):
        kept = lax.reduce_precision(rest, exponent_bits=8, mantissa_bits=7)
        parts.append(kept.astype(low))
        if index < count - 1:
            rest = rest - kept
    return parts


def bdot(left, right):
    return jnp.dot(left, right, preferred_element_type=jnp.float32)


def apply(matrix_parts, operand):
    high, small = matrix_parts
    operand_high, operand_small = split(operand, 2)
    return bdot(high, operand_high) + (bdot(high, operand_small) + bdot(small, operand_high))


def shards(noise, inv_diag, coupling, order):
    block_count = noise.shape[0]
    node_count = noise.shape[1]
    sample_count = noise.shape[2]
    pieces = 2 if sample_count % 256 == 0 else 1
    width = sample_count // pieces
    inv_full = lax.all_gather(inv_diag, "cols", axis=2, tiled=True)
    coupling_parts = [
        split(lax.all_gather(coupling[block], "cols", axis=1, tiled=True), 2)
        for block in range(block_count)
    ]
    driven = [apply(split(inv_full[block], 2), noise[block]) for block in range(block_count)]
    driven_pieces = [
        [driven[block][:, p * width : (p + 1) * width] for p in range(pieces)]
        for block in range(block_count)
    ]

    def chain(entering, piece, skip_last):
        carried = entering
        results = [None] * block_count
        for block in range(block_count - 1, -1, -1):
            if skip_last and block == block_count - 1:
                carried = driven_pieces[block][piece]
            else:
                carried = driven_pieces[block][piece] + apply(coupling_parts[block], carried)
            results[block] = carried
        return results

    first = [shifted(chain(None, p, True)[0], "tm", -1) for p in range(pieces)]

    def relay_step(step, entering):
        return [shifted(chain(entering[p], p, False)[0], "tm", -1) for p in range(pieces)]

    entering = lax.fori_loop(0, lax.axis_size("tm") - 2, relay_step, first)
    finals = [chain(entering[p], p, False) for p in range(pieces)]
    selector = (order[:, None] == jnp.arange(node_count, dtype=order.dtype)[None, :]).astype(low)
    outputs = []
    for block in range(block_count):
        field = jnp.concatenate([finals[p][block] for p in range(pieces)], axis=1)
        top, middle, bottom = split(field, 3)
        outputs.append(bdot(selector, top) + (bdot(selector, middle) + bdot(selector, bottom)))
    return jnp.stack(outputs, axis=0)


def solution(mesh):
    return jax.shard_map(
        shards,
        mesh=mesh,
        in_specs=(
            P(("parts", "tm"), None, "cols"),
            P(("parts", "tm"), None, "cols"),
            P(("parts", "tm"), None, "cols"),
            P(),
        ),
        out_specs=P(("parts", "tm"), None, "cols"),
        check_vma=False,
    )
```

profile of v0, /device:TPU:1, one launch (start us, length us, event | category | flops | bytes accessed | tf_op | source)
XLA Modules:
  0.0 439.5 jit_solution(6839977181822519246)
XLA Ops:
  6.5 3.0 fusion.150
  11.0 81.5 %all-gather.8.cloned.1.call-done = f32[1,1024,1024]{2,1,0:T(8,128)} async-done(((f32[1,1024,256]{2,1,0:T(8,128)}), f32[1,1024,1024]{2,1,0:T(8,128)}) %all-gather.8.cloned.1.call-update) | async-done | bytes 4194320 | tf_op jit(solution)/shard_map/all_gather | solution.py:44
  92.6 4.4 %reduce-precision_convert_fusion.13 = (bf16[1024,1024]{1,0:T(8,128)(2,1)S(1)}, bf16[1024,1024]{1,0:T(8,128)(2,1)}) fusion(f32[1,1024,1024]{2,1,0:T(8,128)} %all-gather.8.cloned.1.call-done), kind=kLoop, calls=%fused_computation.43 | loop fusion | flops 5242880 | bytes 8388608 | tf_op jit(solution)/shard_map/convert_element_type | solution.py:20
  97.0 76.5 %all-gather.10.cloned.1.call-done = f32[1,1024,1024]{2,1,0:T(8,128)} async-done(((f32[1,1024,256]{2,1,0:T(8,128)}), f32[1,1024,1024]{2,1,0:T(8,128)}) %all-gather.10.cloned.1.call-update) | async-done | bytes 4194320 | tf_op jit(solution)/shard_map/all_gather | solution.py:44
  173.5 5.0 %reduce-precision_convert_fusion.12 = (bf16[1024,1024]{1,0:T(8,128)(2,1)}, bf16[1024,1024]{1,0:T(8,128)(2,1)}) fusion(f32[1,1024,1024]{2,1,0:T(8,128)} %all-gather.10.cloned.1.call-done), kind=kLoop, calls=%fused_computation.41 | loop fusion | flops 5242880 | bytes 8388608 | tf_op jit(solution)/shard_map/convert_element_type | solution.py:20
  178.5 144.9 %all-gather.6.cloned.1.call-done = f32[2,1024,1024]{2,1,0:T(8,128)} async-done(((f32[2,1024,256]{2,1,0:T(8,128)}), f32[2,1024,1024]{2,1,0:T(8,128)}) %all-gather.6.cloned.1.call-update) | async-done | bytes 8388624 | tf_op jit(solution)/shard_map/all_gather | solution.py:42
  323.4 3.4 fusion.47
  326.9 3.8 fusion.97
  341.5 2.4 collective-permute-start.2
  343.8 2.1 collective-permute-start.3
  347.0 2.0 copy.10
  349.0 2.0 copy.9
  351.1 2.3 fusion.151
  353.4 4.4 %collective-permute-done.3 = f32[1024,128]{0,1:T(8,128)S(1)} collective-permute-done((f32[1024,128]{0,1:T(8,128)}, f32[1024,128]{0,1:T(8,128)S(1)}, u32[]{:S(2)}, u32[]{:S(2)}) %collective-permute-start.3) | collective-permute-done | bytes 524320 | tf_op jit(solution)/shard_map/ppermute | solution.py:12
  357.8 54.2 %while.12 = (s32[]{:T(128)}, f32[1024,128]{0,1:T(8,128)S(1)}, f32[1024,128]{0,1:T(8,128)S(1)}, bf16[1024,1024]{1,0:T(8,128)(2,1)}, bf16[1024,1024]{1,0:T(8,128)(...) while((s32[]{:T(128)}, f32[1024,128]{0,1:T(8,128)S(1)}, ...), condition=%wide.region_1.0_spmd, body=%wide.region_0.0_spmd.sunk | while | flops 3226992640 | bytes 81789320 | solution.py:69
  357.8 2.5 fusion.228
  366.2 1.9 collective-permute-start
  374.2 1.9 collective-permute-start.1
  376.9 8.0 %collective-permute-done.1 = f32[1024,128]{0,1:T(8,128)S(1)} collective-permute-done((f32[1024,128]{0,1:T(8,128)}, f32[1024,128]{0,1:T(8,128)S(1)}, u32[]{:S(2)}, u32[]{:S(2)}) %collective-permute-start.1) | collective-permute-done | bytes 524320 | tf_op jit(solution)/shard_map/while/body/eval_jaxpr/ppermute | solution.py:12
  384.9 2.5 fusion.228
  393.3 1.9 collective-permute-start
  401.3 1.9 collective-permute-start.1
  404.0 8.0 %collective-permute-done.1 = f32[1024,128]{0,1:T(8,128)S(1)} collective-permute-done((f32[1024,128]{0,1:T(8,128)}, f32[1024,128]{0,1:T(8,128)S(1)}, u32[]{:S(2)}, u32[]{:S(2)}) %collective-permute-start.1) | collective-permute-done | bytes 524320 | tf_op jit(solution)/shard_map/while/body/eval_jaxpr/ppermute | solution.py:12
  412.0 2.6 fusion.136
  (110 shorter events, 56.8 us)
Async XLA Ops:
  6.5 86.0 %all-gather.8.cloned.1.call-start = ((), (), s32[]{:S(2)}) async-start(), calls=%async_computation.1 | async-start | bytes 5242880 | tf_op jit(solution)/shard_map/all_gather | solution.py:44
  9.6 163.9 %all-gather.10.cloned.1.call-start = ((), (), s32[]{:S(2)}) async-start(), calls=%async_computation.2 | async-start | bytes 5242880 | tf_op jit(solution)/shard_map/all_gather | solution.py:44
  10.3 313.1 %all-gather.6.cloned.1.call-start = ((), (), s32[]{:S(2)}) async-start(), calls=%async_computation | async-start | bytes 10485760 | tf_op jit(solution)/shard_map/all_gather | solution.py:42
  323.4 7.2 %copy-start.7 = (f32[2,1024,1024]{2,1,0:T(8,128)S(1)}, f32[2,1024,1024]{2,1,0:T(8,128)}, u32[]{:S(2)}) copy-start(f32[2,1024,1024]{2,1,0:T(8,128)} %all-gather.6.cloned.1.call-done) | copy-start | bytes 25165828
  326.8 4.0 copy-start.14
  331.6 14.3 %copy-start.8 = (f32[1024,256]{0,1:T(8,128)}, f32[1024,256]{0,1:T(8,128)S(1)}, u32[]{:S(2)}) copy-start(f32[1024,256]{0,1:T(8,128)S(1)} %fusion.69) | copy-start | bytes 3145732
  338.1 1.7 copy-start.15
  341.5 11.9 %collective-permute-start.2 = (f32[1024,128]{0,1:T(8,128)}, f32[1024,128]{0,1:T(8,128)S(1)}, u32[]{:S(2)}, u32[]{:S(2)}) collective-permute-start(f32[1024,128]{0,1:T(8,128)} %fusion.71), channel_id=1, source_target_pairs={{4,0},{8,4},{12,8},{5,1},{9,5},{13,9},{6,2},{10,6},{14,10},{7,3},{... | collective-permute-start | bytes 1572872 | tf_op jit(solution)/shard_map/ppermute | solution.py:12
  343.8 14.0 %collective-permute-start.3 = (f32[1024,128]{0,1:T(8,128)}, f32[1024,128]{0,1:T(8,128)S(1)}, u32[]{:S(2)}, u32[]{:S(2)}) collective-permute-start(f32[1024,128]{0,1:T(8,128)} %fusion.74), channel_id=1, source_target_pairs={{4,0},{8,4},{12,8},{5,1},{9,5},{13,9},{6,2},{10,6},{14,10},{7,3},{... | collective-permute-start | bytes 1572872 | tf_op jit(solution)/shard_map/ppermute | solution.py:12
  357.8 2.5 copy-start
  362.9 1.6 copy-start.3
  362.9 1.7 copy-start.13
  364.5 3.6 copy-start.5
  366.2 10.7 %collective-permute-start = (f32[1024,128]{0,1:T(8,128)}, f32[1024,128]{0,1:T(8,128)S(1)}, u32[]{:S(2)}, u32[]{:S(2)}) collective-permute-start(f32[1024,128]{0,1:T(8,128)} %fusion.232), channel_id=1, source_target_pairs={{4,0},{8,4},{12,8},{5,1},{9,5},{13,9},{6,2},{10,6},{14,10},{7,3},{... | collective-permute-start | bytes 1572872 | tf_op jit(solution)/shard_map/while/body/eval_jaxpr/ppermute | solution.py:12
  374.2 10.7 %collective-permute-start.1 = (f32[1024,128]{0,1:T(8,128)}, f32[1024,128]{0,1:T(8,128)S(1)}, u32[]{:S(2)}, u32[]{:S(2)}) collective-permute-start(f32[1024,128]{0,1:T(8,128)} %fusion.238), channel_id=1, source_target_pairs={{4,0},{8,4},{12,8},{5,1},{9,5},{13,9},{6,2},{10,6},{14,10},{7,3},{... | collective-permute-start | bytes 1572872 | tf_op jit(solution)/shard_map/while/body/eval_jaxpr/ppermute | solution.py:12
  384.9 2.5 copy-start
  390.0 1.6 copy-start.3
  390.0 1.7 copy-start.13
  391.6 3.6 copy-start.5
  393.3 10.7 %collective-permute-start = (f32[1024,128]{0,1:T(8,128)}, f32[1024,128]{0,1:T(8,128)S(1)}, u32[]{:S(2)}, u32[]{:S(2)}) collective-permute-start(f32[1024,128]{0,1:T(8,128)} %fusion.232), channel_id=1, source_target_pairs={{4,0},{8,4},{12,8},{5,1},{9,5},{13,9},{6,2},{10,6},{14,10},{7,3},{... | collective-permute-start | bytes 1572872 | tf_op jit(solution)/shard_map/while/body/eval_jaxpr/ppermute | solution.py:12
  401.3 10.7 %collective-permute-start.1 = (f32[1024,128]{0,1:T(8,128)}, f32[1024,128]{0,1:T(8,128)S(1)}, u32[]{:S(2)}, u32[]{:S(2)}) collective-permute-start(f32[1024,128]{0,1:T(8,128)} %fusion.238), channel_id=1, source_target_pairs={{4,0},{8,4},{12,8},{5,1},{9,5},{13,9},{6,2},{10,6},{14,10},{7,3},{... | collective-permute-start | bytes 1572872 | tf_op jit(solution)/shard_map/while/body/eval_jaxpr/ppermute | solution.py:12
  412.0 2.6 copy-start.6
  414.6 1.6 copy-start.1
  419.1 1.6 copy-start.4
  (10 other events, 11.2 us)
Sparse Core Ops, SparseCore 0:
  9.7 82.8 all-gather.7
  94.1 79.2 all-gather.9
  175.0 148.3 all-gather.5
where the time goes:
time: 440 us; the launch traced here: 439 us
  waiting for transfers between devices  326 us (74%)
  matrix products  59.5 us (14%)
  local copies, waits for them, and re-layouts  16.8 us (4%)
  between operations  13.4 us (3%)
  starting transfers between devices  12.2 us (3%)
  other arithmetic  10.9 us (2%)
    all_gather x2, waiting for transfers between devices, shards(): lax.all_gather(coupling[block], 'cols', axis=1, tiled=True)  158 us
    all_gather x1, waiting for transfers between devices, shards(): inv_full = lax.all_gather(inv_diag, 'cols', axis=2, tiled=True)  145 us
    dot_general x54, matrix products, bdot(): return jnp.dot(left, right, preferred_element_type=jnp.float32)  59.5 us
    ppermute x6, waiting for transfers between devices, shifted(): return lax.ppermute(block, axis, route)  22 us
    ppermute x6, starting transfers between devices, shifted(): return lax.ppermute(block, axis, route)  12.1 us
    convert_element_type x2, other arithmetic, split(): parts.append(kept.astype(low))  9.48 us
  transfers between devices with their start and end apart: 9, of which 8 were waited for; matrix products, arithmetic and copies ran while one was open for 6% of the time, Pallas kernels for 0%

commit v1 on v0

--- a/solution.py
+++ b/solution.py
@@ -4,6 +4,12 @@
 from jax.sharding import PartitionSpec as P
 
 low = jnp.bfloat16
+
+
+def laid_out(blocks, dim):
+    shape = list(blocks.shape[1:])
+    shape[dim] *= blocks.shape[0]
+    return jnp.moveaxis(blocks, 0, dim).reshape(shape)
 
 
 def shifted(block, axis, distance):
@@ -39,7 +45,14 @@
     sample_count = noise.shape[2]
     pieces = 2 if sample_count % 256 == 0 else 1
     width = sample_count // pieces
-    inv_full = lax.all_gather(inv_diag, "cols", axis=2, tiled=True)
+    size = lax.axis_size("cols")
+    ahead = [(i_2, (i_2 + 1) % size) for i_2 in range(size)]
+    pieces_2 = [inv_diag]
+    while len(pieces_2) < size:
+        pieces_2.append(lax.ppermute(pieces_2[-1], "cols", ahead))
+    mine = lax.axis_index("cols")
+    pieces_2 = jnp.stack(pieces_2)[(mine - jnp.arange(size)) % size]
+    inv_full = laid_out(pieces_2, 2)
     coupling_parts = [
         split(lax.all_gather(coupling[block], "cols", axis=1, tiled=True), 2)
         for block in range(block_count)

time: 440 us -> 442 us (level)
  the two profiles are of different devices: /device:TPU:1 before, /device:TPU:17 now
where the time goes in v1:
time: 442 us; the launch traced here: 441 us
  waiting for transfers between devices  277 us (63%)
  matrix products  57.8 us (13%)
  local copies, waits for them, and re-layouts  41.5 us (9%)
  starting transfers between devices  28.3 us (6%)
  other arithmetic  22.3 us (5%)
  between operations  13.8 us (3%)
    ppermute x3, waiting for transfers between devices, shards(): pieces_2.append(lax.ppermute(pieces_2[-1], 'cols', ahead))  259 us
    dot_general x54, matrix products, bdot(): return jnp.dot(left, right, preferred_element_type=jnp.float32)  57.8 us
    ppermute x6, starting transfers between devices, shifted(): return lax.ppermute(block, axis, route)  24.6 us
    ppermute x6, waiting for transfers between devices, shifted(): return lax.ppermute(block, axis, route)  17.6 us
    convert_element_type x3, other arithmetic, split(): parts.append(kept.astype(low))  15.2 us
    convert_element_type x4, local copies, waits for them, and re-layouts, split(): parts.append(kept.astype(low))  13.4 us
  transfers between devices with their start and end apart: 11, of which 7 were waited for; matrix products, arithmetic and copies ran while one was open for 17% of the time, Pallas kernels for 0%

profile of v1, /device:TPU:17, one launch (start us, length us, event | category | flops | bytes accessed | tf_op | source)
XLA Modules:
  0.0 440.6 jit_solution(10559998182430874481)
XLA Ops:
  6.5 3.2 fusion.140
  11.2 112.7 %collective-permute-done.2 = f32[2,1024,256]{2,1,0:T(8,128)S(1)} collective-permute-done((f32[2,1024,256]{2,1,0:T(8,128)S(1)}, f32[2,1024,256]{2,1,0:T(8,128)S(1)}, u32[]{:S(2)}, u32[]{:S(2)}) %collective-permute-start.2) | collective-permute-done | bytes 2097184 | tf_op jit(solution)/shard_map/ppermute | solution.py:52
  126.4 44.6 %collective-permute-done.3 = f32[2,1024,256]{2,1,0:T(8,128)} collective-permute-done((f32[2,1024,256]{2,1,0:T(8,128)S(1)}, f32[2,1024,256]{2,1,0:T(8,128)}, u32[]{:S(2)}, u32[]{:S(2)}) %collective-permute-start.3) | collective-permute-done | bytes 2097184 | tf_op jit(solution)/shard_map/ppermute | solution.py:52
  172.1 101.7 %collective-permute-done.4 = f32[2,1024,256]{2,1,0:T(8,128)} collective-permute-done((f32[2,1024,256]{2,1,0:T(8,128)}, f32[2,1024,256]{2,1,0:T(8,128)}, u32[]{:S(2)}, u32[]{:S(2)}) %collective-permute-start.4) | collective-permute-done | bytes 2097184 | tf_op jit(solution)/shard_map/ppermute | solution.py:52
  273.9 5.6 %pad_maximum_fusion = f32[4,2,1024,256]{3,2,1,0:T(8,128)} fusion(f32[1,2,1024,256]{3,2,1,0:T(8,128)} %bitcast.7, f32[1,2,1024,256]{3,2,1,0:T(8,128)} %bitcast.6, f32[1,2,1024,256]{3,2,1,0:T(8,128)} %bitcast.195, f32[1,2,1024,256]{3,2,1,0:T(8,128)S(1)} %bitcast.194), kind=kLoop, calls=%fused_computation.41 | loop fusion | flops 6291456 | bytes 16777216 | tf_op jit(solution)/shard_map/stack | solution.py:54
  279.4 7.7 %gather_fusion = f32[4,2,1024,256]{3,2,1,0:T(8,128)} fusion(f32[4,2,1024,256]{3,2,1,0:T(8,128)} %pad_maximum_fusion, s32[1024]{0:T(1024)S(1)} %pad_clamp_fusion), kind=kCustom, calls=%fused_computation | custom fusion | bytes 16777232 | tf_op jit(solution)/shard_map/gather | solution.py:54
  287.2 7.2 %fusion.33 = (bf16[1,1024,4,256]{3,1,0,2:T(8,128)(2,1)}, bf16[1,1024,4,256]{3,1,0,2:T(8,128)(2,1)}, bf16[1,1024,4,256]{3,1,0,2:T(8,128)(2,1)}, bf16[1,1024,4,256]{3,1,0,2:T(8,128)(2,1)S(1)}) fusion(f32[2,1024,4,256]{3,1,0,2:T(8,128)} %bitcast.187), kind=kLoop, calls=%fused_computation.51 | loop fusion | flops 10485760 | bytes 16777216 | tf_op jit(solution)/shard_map/convert_element_type | solution.py:26
  294.3 4.0 copy.21
  298.3 4.0 copy.22
  302.3 2.5 copy.19
  304.8 3.0 copy.20
  307.8 2.8 fusion.101
  319.0 2.9 reduce-precision_convert_fusion.13
  325.6 15.1 %collective-permute-start.6 = (f32[1024,128]{0,1:T(8,128)}, f32[1024,128]{0,1:T(8,128)S(1)}, u32[]{:S(2)}, u32[]{:S(2)}) collective-permute-start(f32[1024,128]{0,1:T(8,128)} %fusion.64), channel_id=1, source_target_pairs={{4,0},{8,4},{12,8},{5,1},{9,5},{13,9},{6,2},{10,6},{14,10},{7,3},{... | collective-permute-start | bytes 1572872 | tf_op jit(solution)/shard_map/ppermute | solution.py:18
  345.1 1.9 collective-permute-start.5
  348.1 2.0 copy.25
  350.2 2.1 copy.26
  352.2 5.1 %reduce-precision_convert_fusion.12 = (bf16[1024,1024]{1,0:T(8,128)(2,1)}, bf16[1024,1024]{1,0:T(8,128)(2,1)}) fusion(f32[1,1024,1024]{2,1,0:T(8,128)} %all-gather.7.cloned.1.call-done), kind=kLoop, calls=%fused_computation.43 | loop fusion | flops 5242880 | bytes 8388608 | tf_op jit(solution)/shard_map/convert_element_type | solution.py:26
  357.4 55.5 %while.12 = (s32[]{:T(128)}, f32[1024,128]{0,1:T(8,128)S(1)}, f32[1024,128]{0,1:T(8,128)S(1)}, bf16[1024,1024]{1,0:T(8,128)(2,1)}, bf16[1024,1024]{1,0:T(8,128)(...) while((s32[]{:T(128)}, f32[1024,128]{0,1:T(8,128)S(1)}, ...), condition=%wide.region_1.2_spmd, body=%wide.region_0.1_spmd.sunk | while | flops 3226992640 | bytes 81789320 | solution.py:82
  357.4 2.5 fusion.229
  377.1 8.0 %collective-permute-done = f32[1024,128]{0,1:T(8,128)S(1)} collective-permute-done((f32[1024,128]{0,1:T(8,128)}, f32[1024,128]{0,1:T(8,128)S(1)}, u32[]{:S(2)}, u32[]{:S(2)}) %collective-permute-start) | collective-permute-done | bytes 524320 | tf_op jit(solution)/shard_map/while/body/eval_jaxpr/ppermute | solution.py:18
  385.1 2.4 fusion.229
  404.8 8.0 %collective-permute-done = f32[1024,128]{0,1:T(8,128)S(1)} collective-permute-done((f32[1024,128]{0,1:T(8,128)}, f32[1024,128]{0,1:T(8,128)S(1)}, u32[]{:S(2)}, u32[]{:S(2)}) %collective-permute-start) | collective-permute-done | bytes 524320 | tf_op jit(solution)/shard_map/while/body/eval_jaxpr/ppermute | solution.py:18
  412.8 2.6 fusion.122
  (132 shorter events, 75.0 us)
Async XLA Ops:
  6.5 3.3 copy-start.20
  6.5 312.4 %all-gather.5.cloned.1.call-start = ((), (), s32[]{:S(2)}) async-start(), calls=%async_computation | async-start | bytes 5242880 | tf_op jit(solution)/shard_map/all_gather | solution.py:57
  9.8 342.5 %all-gather.7.cloned.1.call-start = ((), (), s32[]{:S(2)}) async-start(), calls=%async_computation.1 | async-start | bytes 5242880 | tf_op jit(solution)/shard_map/all_gather | solution.py:57
  9.8 114.1 %collective-permute-start.2 = (f32[2,1024,256]{2,1,0:T(8,128)S(1)}, f32[2,1024,256]{2,1,0:T(8,128)S(1)}, u32[]{:S(2)}, u32[]{:S(2)}) collective-permute-start(f32[2,1024,256]{2,1,0:T(8,128)S(1)} %copy-done.20), channel_id=1, source_target_pairs={{0,1},{1,2},{2,3},{3,0},{4,5},{5,6},{6,7},{7,4},{8,9},{9,10},{10,1... | collective-permute-start | bytes 6291464 | tf_op jit(solution)/shard_map/ppermute | solution.py:52
  125.2 45.8 %collective-permute-start.3 = (f32[2,1024,256]{2,1,0:T(8,128)S(1)}, f32[2,1024,256]{2,1,0:T(8,128)}, u32[]{:S(2)}, u32[]{:S(2)}) collective-permute-start(f32[2,1024,256]{2,1,0:T(8,128)S(1)} %collective-permute-done.2), channel_id=1, source_target_pairs={{0,1},{1,2},{2,3},{3,0},{4,5},{5,6},{6,7},{7,4},{8,9},{9,10},{10,1... | collective-permute-start | bytes 6291464 | tf_op jit(solution)/shard_map/ppermute | solution.py:52
  171.0 102.9 %collective-permute-start.4 = (f32[2,1024,256]{2,1,0:T(8,128)}, f32[2,1024,256]{2,1,0:T(8,128)}, u32[]{:S(2)}, u32[]{:S(2)}) collective-permute-start(f32[2,1024,256]{2,1,0:T(8,128)} %collective-permute-done.3), channel_id=1, source_target_pairs={{0,1},{1,2},{2,3},{3,0},{4,5},{5,6},{6,7},{7,4},{8,9},{9,10},{10,1... | collective-permute-start | bytes 6291464 | tf_op jit(solution)/shard_map/ppermute | solution.py:52
  307.8 2.8 copy-start.18
  307.8 3.2 copy-start.19
  313.3 10.3 %copy-start.7 = (f32[1024,256]{0,1:T(8,128)}, f32[1024,256]{0,1:T(8,128)S(1)}, u32[]{:S(2)}) copy-start(f32[1024,256]{0,1:T(8,128)S(1)} %fusion.58) | copy-start | bytes 3145732
  313.3 2.3 copy-start.17
  321.9 18.8 %copy-start.2 = (bf16[1024,1024]{1,0:T(8,128)(2,1)}, bf16[1024,1024]{1,0:T(8,128)(2,1)S(1)}, u32[]{:S(2)}) copy-start(bf16[1024,1024]{1,0:T(8,128)(2,1)S(1)} %get-tuple-element.208) | copy-start | bytes 6291460
  325.6 17.0 %copy-start.8 = (f32[1024,256]{0,1:T(8,128)S(1)}, f32[1024,256]{0,1:T(8,128)}, u32[]{:S(2)}) copy-start(f32[1024,256]{0,1:T(8,128)} %copy-done.7) | copy-start | bytes 3145732
  325.6 31.7 %collective-permute-start.6 = (f32[1024,128]{0,1:T(8,128)}, f32[1024,128]{0,1:T(8,128)S(1)}, u32[]{:S(2)}, u32[]{:S(2)}) collective-permute-start(f32[1024,128]{0,1:T(8,128)} %fusion.64), channel_id=1, source_target_pairs={{4,0},{8,4},{12,8},{5,1},{9,5},{13,9},{6,2},{10,6},{14,10},{7,3},{... | collective-permute-start | bytes 1572872 | tf_op jit(solution)/shard_map/ppermute | solution.py:18
  345.1 12.2 %collective-permute-start.5 = (f32[1024,128]{0,1:T(8,128)}, f32[1024,128]{0,1:T(8,128)S(1)}, u32[]{:S(2)}, u32[]{:S(2)}) collective-permute-start(f32[1024,128]{0,1:T(8,128)} %fusion.61), channel_id=1, source_target_pairs={{4,0},{8,4},{12,8},{5,1},{9,5},{13,9},{6,2},{10,6},{14,10},{7,3},{... | collective-permute-start | bytes 1572872 | tf_op jit(solution)/shard_map/ppermute | solution.py:18
  357.4 2.5 copy-start.5
  359.8 1.7 copy-start.13
  363.1 1.7 copy-start.14
  366.4 10.7 %collective-permute-start.1 = (f32[1024,128]{0,1:T(8,128)}, f32[1024,128]{0,1:T(8,128)S(1)}, u32[]{:S(2)}, u32[]{:S(2)}) collective-permute-start(f32[1024,128]{0,1:T(8,128)} %fusion.234), channel_id=1, source_target_pairs={{4,0},{8,4},{12,8},{5,1},{9,5},{13,9},{6,2},{10,6},{14,10},{7,3},{... | collective-permute-start | bytes 1572872 | tf_op jit(solution)/shard_map/while/body/eval_jaxpr/ppermute | solution.py:18
  374.4 10.7 %collective-permute-start = (f32[1024,128]{0,1:T(8,128)}, f32[1024,128]{0,1:T(8,128)S(1)}, u32[]{:S(2)}, u32[]{:S(2)}) collective-permute-start(f32[1024,128]{0,1:T(8,128)} %fusion.228), channel_id=1, source_target_pairs={{4,0},{8,4},{12,8},{5,1},{9,5},{13,9},{6,2},{10,6},{14,10},{7,3},{... | collective-permute-start | bytes 1572872 | tf_op jit(solution)/shard_map/while/body/eval_jaxpr/ppermute | solution.py:18
  385.1 2.5 copy-start.5
  390.8 1.7 copy-start.14
  394.1 10.7 %collective-permute-start.1 = (f32[1024,128]{0,1:T(8,128)}, f32[1024,128]{0,1:T(8,128)S(1)}, u32[]{:S(2)}, u32[]{:S(2)}) collective-permute-start(f32[1024,128]{0,1:T(8,128)} %fusion.234), channel_id=1, source_target_pairs={{4,0},{8,4},{12,8},{5,1},{9,5},{13,9},{6,2},{10,6},{14,10},{7,3},{... | collective-permute-start | bytes 1572872 | tf_op jit(solution)/shard_map/while/body/eval_jaxpr/ppermute | solution.py:18
  402.1 10.7 %collective-permute-start = (f32[1024,128]{0,1:T(8,128)}, f32[1024,128]{0,1:T(8,128)S(1)}, u32[]{:S(2)}, u32[]{:S(2)}) collective-permute-start(f32[1024,128]{0,1:T(8,128)} %fusion.228), channel_id=1, source_target_pairs={{4,0},{8,4},{12,8},{5,1},{9,5},{13,9},{6,2},{10,6},{14,10},{7,3},{... | collective-permute-start | bytes 1572872 | tf_op jit(solution)/shard_map/while/body/eval_jaxpr/ppermute | solution.py:18
  412.8 2.6 copy-start.1
  (17 other events, 22.8 us)
Sparse Core Ops, SparseCore 0:
  9.9 115.4 all-gather.4
  172.2 116.3 all-gather.6
